TPU v7x, 32 devices: a whole 2x2x4 slice. The times are simulated.
32 devices in a mesh: groups: 1, blk: 8 (over z, y), seg: 2 (over x), freq: 2 (over core).
Axes of the slice: x: 2, y: 2, z: 4, core: 2. Of those that a mesh axis runs over, the one named last changes fastest.
Arguments:
- raw: bfloat16 [64, 64, 16384], P(('groups', 'blk'), 'seg', 'freq'), may hold values from -6 to 6
- taps: float32 [128], replicated, may hold values from -0.5 to 0.5
- send_list: int32 [8, 8, 2], P(('groups', 'blk')), may hold values from 0 to 8, as said below
- recv_row: int32 [8, 8, 2], P(('groups', 'blk')), may hold values from 0 to 16, as said below
Outputs:
- cross_spectra: float32 [2, 256, 128, 128], P(None, ('seg', 'freq'), ('groups', 'blk'))
Inputs may be any that keep to these rules, and one draw needn't show every extreme that they name: send_list[s, o, k] is the local sensing point of source s that goes to owner o in slot k, or 8 for an empty slot; a source names each of its points at most once; the filled slots of a pair come first; some source fills all 2 slots to one owner. recv_row[o, s, k] is the row of owner o that receives slot k of source s, and it is 16 exactly where send_list[s, o, k] is 8; an owner's filled rows are 0 to its count - 1, each once, rising with source and then slot; some owner holds exactly 16 rows.
All inputs are finite; a program needn't handle non-finite values.
Results may differ from a plain program's by a relative error of at most 0.0029.
Values may be sent and summed in bfloat16 or wider, within the bound.
No kernel may reach another device: no remote copies, remote signals or barrier semaphores. Data moves between devices by JAX's collectives and lax.ppermute only.
A program may use at most 128 MiB of HBM per device.

v0:
```python
import math
import jax
import jax.numpy as jnp
from jax import lax
from jax.sharding import PartitionSpec as P

SEG_LEN = 16384
BINS = 256
BAND_LO = 128
HW = 4
OWN = 16
WHITEN_FLOOR = 0.25
TWO_PI = 2.0 * math.pi


def swapped(value, axis, distance):
    mask = 2**distance
    pairs = [(source, source ^ mask) for source in range(lax.axis_size(axis))]
    return lax.ppermute(value, axis, pairs)


def dft_tables(band_index, sample_index):
    wavenumber = BAND_LO + band_index
    phase_int = wavenumber[:, None] * sample_index[None, :] % SEG_LEN
    angles = phase_int.astype(jnp.float32) * (TWO_PI / SEG_LEN)
    norm_scale = 1.0 / math.sqrt(SEG_LEN)
    cos_part = (jnp.cos(angles) * norm_scale).astype(jnp.bfloat16)
    sin_part = (-jnp.sin(angles) * norm_scale).astype(jnp.bfloat16)
    return (cos_part, sin_part)


def dft_tables_fast(band_index, first_sample, count):
    lanes = 128
    wavenumber = BAND_LO + band_index
    coarse = first_sample + lanes * jnp.arange(count // lanes, dtype=jnp.int32)
    fine = jnp.arange(lanes, dtype=jnp.int32)
    coarse_angle = (wavenumber[:, None] * coarse[None, :] % SEG_LEN).astype(jnp.float32) * (
        TWO_PI / SEG_LEN
    )
    fine_angle = (wavenumber[:, None] * fine[None, :] % SEG_LEN).astype(jnp.float32) * (
        TWO_PI / SEG_LEN
    )
    cos_a = jnp.cos(coarse_angle)[:, :, None]
    sin_a = jnp.sin(coarse_angle)[:, :, None]
    cos_b = jnp.cos(fine_angle)[:, None, :]
    sin_b = jnp.sin(fine_angle)[:, None, :]
    norm_scale = 1.0 / math.sqrt(SEG_LEN)
    cos_sum = cos_a * cos_b - sin_a * sin_b
    sin_sum = sin_a * cos_b + cos_a * sin_b
    rows = band_index.shape[0]
    cos_part = (cos_sum * norm_scale).astype(jnp.bfloat16).reshape(rows, count)
    sin_part = (-sin_sum * norm_scale).astype(jnp.bfloat16).reshape(rows, count)
    return (cos_part, sin_part)


def response(band_index, taps):
    wavenumber = BAND_LO + band_index
    lag_index = jnp.arange(taps.shape[0], dtype=jnp.int32)
    phase_int = wavenumber[:, None] * lag_index[None, :] % SEG_LEN
    angles = phase_int.astype(jnp.float32) * (TWO_PI / SEG_LEN)
    real_part = jnp.dot(jnp.cos(angles), taps, precision=lax.Precision.HIGHEST)
    imag_part = jnp.dot(-jnp.sin(angles), taps, precision=lax.Precision.HIGHEST)
    return (real_part, imag_part)


def per_device(raw, taps, send_list, recv_row):
    owners_count = lax.axis_size("blk")
    seg_count = lax.axis_size("seg")
    freq_count = lax.axis_size("freq")
    freq_rank = lax.axis_index("freq")
    sections, seg_dev, half_len = raw.shape
    records = raw.reshape(sections * seg_dev, half_len)
    device_bins = BINS // freq_count
    block_bins = device_bins // seg_count
    capacity = send_list.shape[2]

    def band_of(row_ids):
        owner_core = row_ids // device_bins
        local_row = row_ids % device_bins
        return (
            local_row // block_bins * freq_count + owner_core
        ) * block_bins + local_row % block_bins

    band_rows = band_of(jnp.arange(device_bins * freq_count, dtype=jnp.int32))
    cos_part, sin_part = dft_tables_fast(band_rows, freq_rank * half_len, half_len)
    contract = (((1,), (1,)), ((), ()))
    real_all = lax.dot_general(cos_part, records, contract, preferred_element_type=jnp.float32)
    imag_all = lax.dot_general(sin_part, records, contract, preferred_element_type=jnp.float32)
    blocks = jnp.stack([real_all, imag_all], axis=1)
    blocks = blocks.reshape(freq_count, device_bins, 2, records.shape[0])
    if freq_count == 2:
        kept = jnp.where(freq_rank == 0, blocks[0], blocks[1])
        sent = jnp.where(freq_rank == 0, blocks[1], blocks[0])
        spectra = kept + swapped(sent, "freq", 0)
    else:
        spectra = lax.psum_scatter(
            blocks.reshape(device_bins * freq_count, 2, records.shape[0]),
            "freq",
            scatter_dimension=0,
            tiled=True,
        )
    real_part = spectra[:, 0]
    imag_part = spectra[:, 1]
    amplitude = jnp.sqrt(real_part * real_part + imag_part * imag_part + 1e-06)
    amp_blocks = amplitude.reshape(seg_count, block_bins, -1)
    band_rims = jnp.stack([amp_blocks[:, :HW], amp_blocks[:, block_bins - HW :]])
    partner = swapped(band_rims, "freq", 0)
    zero_rim = jnp.zeros_like(partner[1][:1])
    right_prev = jnp.concatenate([zero_rim, partner[1][:-1]], axis=0)
    left_next = jnp.concatenate([partner[0][1:], zero_rim], axis=0)
    first_core = freq_rank == 0
    lower_rim = jnp.where(first_core, right_prev, partner[1])
    upper_rim = jnp.where(first_core, partner[0], left_next)
    padded = jnp.concatenate([lower_rim, amp_blocks, upper_rim], axis=1)
    window_sum = padded[:, 0:block_bins]
    for offset_step in range(1, 2 * HW + 1):
        window_sum = window_sum + padded[:, offset_step : offset_step + block_bins]
    span_ids = jnp.arange(seg_count, dtype=jnp.int32)[:, None]
    offsets = jnp.arange(block_bins, dtype=jnp.int32)[None, :]
    position = (span_ids * freq_count + freq_rank) * block_bins + offsets
    counted = jnp.minimum(position + HW, BINS - 1) - jnp.maximum(position - HW, 0) + 1
    smooth = window_sum / counted.astype(jnp.float32)[:, :, None]
    divisor = jnp.maximum(smooth, WHITEN_FLOOR).reshape(device_bins, -1)
    local_bins = freq_rank * device_bins + jnp.arange(device_bins, dtype=jnp.int32)
    response_re, response_im = response(band_of(local_bins), taps)
    scaled_re = real_part / divisor
    scaled_im = imag_part / divisor
    white_re = scaled_re * response_re[:, None] - scaled_im * response_im[:, None]
    white_im = scaled_re * response_im[:, None] + scaled_im * response_re[:, None]
    whitened = jnp.stack([white_re, white_im], axis=1).astype(jnp.bfloat16)
    whitened = whitened.reshape(device_bins, 2, sections, seg_dev)
    slot_ids = send_list.reshape(-1)
    picker = (slot_ids[:, None] == jnp.arange(sections, dtype=jnp.int32)[None, :]).astype(
        jnp.bfloat16
    )
    packed = jnp.einsum(
        "pc,fxcn->pxnf", picker, whitened, preferred_element_type=jnp.float32
    ).astype(jnp.bfloat16)
    packed = packed.reshape(owners_count, capacity, 2, seg_dev, device_bins)
    arrived = lax.all_to_all(packed, "blk", split_axis=0, concat_axis=0, tiled=True)
    arrived = arrived.reshape(owners_count * capacity, 2, seg_dev, device_bins)
    row_targets = recv_row.reshape(-1)
    placer = (jnp.arange(OWN, dtype=jnp.int32)[:, None] == row_targets[None, :]).astype(
        jnp.bfloat16
    )
    own_block = jnp.einsum(
        "rp,pxnf->xnrf", placer, arrived, preferred_element_type=jnp.float32
    ).astype(jnp.bfloat16)
    incoming = lax.all_gather(own_block, "blk", axis=2, tiled=True)
    cross_re = jnp.einsum("xnif,xnjf->fij", own_block, incoming, preferred_element_type=jnp.float32)
    cross_im = jnp.einsum(
        "nif,njf->fij", own_block[1], incoming[0], preferred_element_type=jnp.float32
    )
    cross_im = cross_im - jnp.einsum(
        "nif,njf->fij", own_block[0], incoming[1], preferred_element_type=jnp.float32
    )
    pair_block = jnp.stack([cross_re, cross_im])
    stacked = lax.psum_scatter(pair_block, "seg", scatter_dimension=1, tiled=True)
    return stacked / jnp.float32(seg_dev * seg_count)


def solution(mesh):
    placed = (
        P(("groups", "blk"), "seg", "freq"),
        P(),
        P(("groups", "blk"), None, None),
        P(("groups", "blk"), None, None),
    )
    return jax.shard_map(
        per_device,
        mesh=mesh,
        in_specs=placed,
        out_specs=P(None, ("seg", "freq"), ("groups", "blk"), None),
        check_vma=False,
    )
```

profile of v0, /device:TPU:0, one launch (start us, length us, event | category | flops | bytes accessed | tf_op | source)
XLA Modules:
  0.0 164.3 jit_solution(13299411521968200792)
XLA Ops:
  6.6 0.6 fusion.52
  7.2 0.6 fusion.54
  7.8 5.0 %multiply_convert_fusion.1 = (bf16[256,64,128]{2,1,0:T(8,128)(2,1)S(1)}, bf16[256,64,128]{2,1,0:T(8,128)(2,1)S(1)}) fusion(f32[256,128]{1,0:T(8,128)S(1)} %get-tuple-element.22, f32[256,64]{1,0:T(8,128)S(1)} %get-tuple-element.20, f32[256,128]{1,0:T(8,128)S(1)} %get-tuple-element.21, f32[256,64]{1,0:T(8,128)S(1)} %get-tuple-element.19), kind=kLoop, calls=%fused_computation.1 | loop fusion | flops 23068672 | bytes 8781824 | tf_op jit(solution)/shard_map/convert_element_type | solution.py:51
  12.7 2.9 %fusion.8 = f32[256,1,256]{0,2,1:T(8,128)S(1)} fusion(bf16[256,8192]{1,0:T(8,128)(2,1)S(1)} %bitcast.112, bf16[32,8,64,128]{3,2,1,0:T(8,128)(2,1)S(1)} %bitcast.102), kind=kOutput, calls=%fused_computation.16 | convolution fusion | flops 1073741824 | bytes 8650752 | tf_op jit(solution)/shard_map/dot_general | solution.py:87
  15.6 2.9 %fusion.11 = f32[256,1,256]{0,2,1:T(8,128)S(1)} fusion(bf16[256,8192]{1,0:T(8,128)(2,1)S(1)} %bitcast.113, bf16[32,8,64,128]{3,2,1,0:T(8,128)(2,1)S(1)} %bitcast.101), kind=kOutput, calls=%fused_computation.17 | convolution fusion | flops 1073741824 | bytes 8650752 | tf_op jit(solution)/shard_map/dot_general | solution.py:88
  22.4 1.0 copy.38
  23.4 7.2 %all-to-all-start = ((bf16[8,2,2,32,128]{4,1,3,2,0:T(2,128)(2,1)}), bf16[8,2,2,32,128]{4,1,3,2,0:T(2,128)(2,1)S(1)}, u32[]{:S(2)}, u32[]{:S(2)}) async-start(bf16[8,2,2,32,128]{4,1,3,2,0:T(2,128)(2,1)} %copy.38), calls=%async_computation | async-start | bytes 524288 | tf_op jit(solution)/shard_map/all_to_all | solution.py:140
  30.8 9.0 %all-to-all-done = bf16[8,2,2,32,128]{4,1,3,2,0:T(2,128)(2,1)S(1)} async-done(((bf16[8,2,2,32,128]{4,1,3,2,0:T(2,128)(2,1)}), bf16[8,2,2,32,128]{4,1,3,2,0:T(2,128)(2,1)S(1)}, u32[]{:S(2)}, u32[]{:S(2)}) %all-to-all-start) | async-done | bytes 262176 | tf_op jit(solution)/shard_map/all_to_all | solution.py:140
  40.0 0.9 fusion.7
  41.2 2.7 %copy.41 = bf16[2,32,16,128]{1,2,0,3:T(8,128)(2,1)S(1)} copy(bf16[2,32,16,128]{3,2,1,0:T(8,128)(2,1)} %fusion.7) | data formatting | bytes 524288 | tf_op jit(solution)/shard_map/convert_element_type | solution.py:148
  43.8 1.0 slice_bitcast_fusion.2
  44.8 1.2 copy.45
  46.1 1.2 copy.43
  47.3 43.8 %all-gather.2.cloned.1.call-done = bf16[2,32,128,128]{3,2,1,0:T(8,128)(2,1)} async-done(((bf16[2,32,16,128]{3,2,1,0:T(8,128)(2,1)}), bf16[2,32,128,128]{3,2,1,0:T(8,128)(2,1)}) %all-gather.2.cloned.1.call-update) | async-done | bytes 2097168 | tf_op jit(solution)/shard_map/all_gather | solution.py:149
  91.2 3.1 %slice_bitcast_fusion = (bf16[32,128,128]{2,1,0:T(8,128)(2,1)}, bf16[32,128,128]{2,1,0:T(8,128)(2,1)}) fusion(bf16[2,32,128,128]{3,2,1,0:T(8,128)(2,1)} %all-gather.2.cloned.1.call-done), kind=kLoop, calls=%fused_computation.20 | loop fusion | bytes 4194304 | tf_op jit(solution)/shard_map/squeeze | solution.py:155
  94.3 2.8 %copy.46 = bf16[32,128,128]{1,0,2:T(8,128)(2,1)} copy(bf16[32,128,128]{2,1,0:T(8,128)(2,1)} %get-tuple-element.5) | data formatting | bytes 2097152 | tf_op jit(solution)/shard_map/squeeze | solution.py:155
  97.1 2.6 %copy.44 = bf16[32,128,128]{1,0,2:T(8,128)(2,1)} copy(bf16[32,128,128]{2,1,0:T(8,128)(2,1)} %get-tuple-element.6) | data formatting | bytes 2097152 | tf_op jit(solution)/shard_map/squeeze | solution.py:152
  99.7 2.8 %fusion.85 = f32[128,16,128]{2,1,0:T(8,128)} fusion(bf16[32,16,128]{0,1,2:T(8,128)(2,1)} %copy.43, bf16[32,128,128]{1,0,2:T(8,128)(2,1)} %copy.44), kind=kOutput, calls=%fused_computation.159 | convolution fusion | flops 16777216 | bytes 2228224 | tf_op jit(solution)/shard_map/nif,njf->fij/dot_general | solution.py:151
  102.5 12.6 %copy.42 = bf16[2,32,128,128]{1,2,0,3:T(8,128)(2,1)} copy(bf16[2,32,128,128]{3,2,1,0:T(8,128)(2,1)S(1)} %copy-done.1) | data formatting | bytes 4194304 | tf_op jit(solution)/shard_map/all_gather | solution.py:149
  115.1 5.8 %convolution_bitcast_fusion = f32[1,128,16,128]{3,2,1,0:T(8,128)S(1)} fusion(bf16[2,32,16,128]{1,2,0,3:T(8,128)(2,1)S(1)} %copy.41, bf16[2,32,128,128]{1,2,0,3:T(8,128)(2,1)} %copy.42), kind=kOutput, calls=%fused_computation.12 | convolution fusion | flops 33554432 | bytes 3407872 | tf_op jit(solution)/shard_map/xnif,xnjf->fij/dot_general | solution.py:150
  121.8 3.0 %copy.70 = f32[16,8,32,128]{3,1,2,0:T(8,128)} copy(f32[16,8,32,128]{3,2,1,0:T(8,128)S(1)} %bitcast.100) | data formatting | bytes 4194304
  124.8 30.2 %reduce-scatter.5.cloned.1.call-done = f32[64,4096]{1,0:T(8,128)} async-done(((f32[128,4096]{1,0:T(8,128)}), f32[64,4096]{1,0:T(8,128)}) %reduce-scatter.5.cloned.1.call-update) | async-done | bytes 1048592
  155.0 1.4 copy.55
  156.4 1.1 copy_multiply_fusion
  (53 shorter events, 5.4 us)
Async XLA Ops:
  6.5 12.6 %copy-start = (f32[128]{0:T(128)S(1)}, f32[128]{0:T(128)}, u32[]{:S(2)}) copy-start(f32[128]{0:T(128)} %param.5) | copy-start | bytes 1540
  7.8 5.0 %copy-start.7 = (bf16[8,32,8192]{2,1,0:T(8,128)(2,1)S(1)}, bf16[8,32,8192]{2,1,0:T(8,128)(2,1)}, u32[]{:S(2)}) copy-start(bf16[8,32,8192]{2,1,0:T(8,128)(2,1)} %param.4) | copy-start | bytes 12582916
  15.6 5.8 %copy-start.5 = (s32[1,8,2]{1,2,0:T(2,128)S(1)}, s32[1,8,2]{1,2,0:T(2,128)}, u32[]{:S(2)}) copy-start(s32[1,8,2]{1,2,0:T(2,128)} %param.6) | copy-start | bytes 196
  18.5 12.1 %copy-start.6 = (s32[1,8,2]{1,2,0:T(2,128)S(1)}, s32[1,8,2]{1,2,0:T(2,128)}, u32[]{:S(2)}) copy-start(s32[1,8,2]{1,2,0:T(2,128)} %param.7) | copy-start | bytes 196
  18.6 1.7 %collective-permute-start = (f32[128,2,256]{0,2,1:T(8,128)S(1)}, f32[128,2,256]{0,2,1:T(8,128)S(1)}, u32[]{:S(2)}, u32[]{:S(2)}) collective-permute-start(f32[128,2,256]{0,2,1:T(8,128)S(1)} %broadcast_select_fusion), channel_id=1, source_target_pairs={{0,1},{1,0},{2,3},{3,2},{4,5},{5,4},{6,7},{7,6},{8,9},{9,8},{10,11... | collective-permute-start | bytes 786440 | tf_op jit(solution)/shard_map/ppermute | solution.py:19
  20.5 1.3 collective-permute-start.1
  23.4 16.4 %all-to-all-start = ((bf16[8,2,2,32,128]{4,1,3,2,0:T(2,128)(2,1)}), bf16[8,2,2,32,128]{4,1,3,2,0:T(2,128)(2,1)S(1)}, u32[]{:S(2)}, u32[]{:S(2)}) async-start(bf16[8,2,2,32,128]{4,1,3,2,0:T(2,128)(2,1)} %copy.38), calls=%async_computation | async-start | bytes 524288 | tf_op jit(solution)/shard_map/all_to_all | solution.py:140
  30.6 60.6 %all-gather.2.cloned.1.call-start = ((), (), s32[]{:S(2)}) async-start(), calls=%async_computation.2 | async-start | bytes 2359296 | tf_op jit(solution)/shard_map/all_gather | solution.py:149
  40.9 114.1 %reduce-scatter.5.cloned.1.call-start = ((), (), s32[]{:S(2)}) async-start(), calls=%async_computation.3 | async-start | bytes 3145728
  94.3 8.3 %copy-start.1 = (bf16[2,32,128,128]{3,2,1,0:T(8,128)(2,1)S(1)}, bf16[2,32,128,128]{3,2,1,0:T(8,128)(2,1)}, u32[]{:S(2)}) copy-start(bf16[2,32,128,128]{3,2,1,0:T(8,128)(2,1)} %all-gather.2.cloned.1.call-done) | copy-start | bytes 6291460
  115.1 5.8 %copy-start.2 = (bf16[32,128,128]{1,0,2:T(8,128)(2,1)S(1)}, bf16[32,128,128]{1,0,2:T(8,128)(2,1)}, u32[]{:S(2)}) copy-start(bf16[32,128,128]{1,0,2:T(8,128)(2,1)} %copy.46) | copy-start | bytes 3145732
  115.1 5.8 %copy-start.3 = (f32[128,16,128]{2,1,0:T(8,128)S(1)}, f32[128,16,128]{2,1,0:T(8,128)}, u32[]{:S(2)}) copy-start(f32[128,16,128]{2,1,0:T(8,128)} %fusion.85) | copy-start | bytes 3145732
  115.1 5.8 %copy-start.4 = (bf16[32,16,128]{0,1,2:T(8,128)(2,1)S(1)}, bf16[32,16,128]{0,1,2:T(8,128)(2,1)}, u32[]{:S(2)}) copy-start(bf16[32,16,128]{0,1,2:T(8,128)(2,1)} %copy.45) | copy-start | bytes 393220
Sparse Core Ops, SparseCore 0:
  41.0 50.0 all-gather.1
  125.0 29.9 reduce-scatter.4
where the time goes:
time: 165 us; the launch traced here: 164 us
  waiting for transfers between devices  83.7 us (51%)
  local copies, waits for them, and re-layouts  33.8 us (20%)
  matrix products  16.9 us (10%)
  between operations  13.6 us (8%)
  starting transfers between devices  8.39 us (5%)
  other arithmetic  7.81 us (5%)
    all_gather x1, waiting for transfers between devices, per_device(): incoming = lax.all_gather(own_block, 'blk', axis=2, tiled=True)  43.8 us
    unnamed x3, waiting for transfers between devices  30.2 us
    all_gather x1, local copies, waits for them, and re-layouts, per_device(): incoming = lax.all_gather(own_block, 'blk', axis=2, tiled=True)  12.6 us
    all_to_all x1, waiting for transfers between devices, per_device(): lax.all_to_all(packed, 'blk', split_axis=0, concat_axis=0, tiled=True)  9.02 us
    all_to_all x1, starting transfers between devices, per_device(): lax.all_to_all(packed, 'blk', split_axis=0, concat_axis=0, tiled=True)  7.18 us
    squeeze x2, local copies, waits for them, and re-layouts, per_device(): incoming[1]  5.95 us
    dot_general x1, matrix products, per_device(): jnp.einsum('xnif,xnjf->fij', own_block, incoming, preferred_element_type=...  5.79 us
    unnamed x21, local copies, waits for them, and re-layouts  4.96 us
  transfers between devices with their start and end apart: 5, of which 5 were waited for; matrix products, arithmetic and copies ran while one was open for 5% of the time, Pallas kernels for 0%

commit v1 on v0

--- a/solution.py
+++ b/solution.py
@@ -11,6 +11,27 @@
 OWN = 16
 WHITEN_FLOOR = 0.25
 TWO_PI = 2.0 * math.pi
+
+
+def ring_gather(x, axis, dim):
+    size, index, rows = (lax.axis_size(axis), lax.axis_index(axis), x.shape[dim])
+    upward = [(i, (i + 1) % size) for i in range(size)]
+    backward = [(i, (i - 1) % size) for i in range(size)]
+    result = jnp.zeros((*x.shape[:dim], size * rows, *x.shape[dim + 1 :]), x.dtype)
+    result = lax.dynamic_update_slice_in_dim(result, x, index * rows, axis=dim)
+    from_left = from_right = x
+    halfway = size // 2
+    for step in range(1, halfway + 1):
+        from_left = lax.ppermute(from_left, axis, upward)
+        result = lax.dynamic_update_slice_in_dim(
+            result, from_left, (index - step) % size * rows, axis=dim
+        )
+        if step < size - halfway:
+            from_right = lax.ppermute(from_right, axis, backward)
+            result = lax.dynamic_update_slice_in_dim(
+                result, from_right, (index + step) % size * rows, axis=dim
+            )
+    return result
 
 
 def swapped(value, axis, distance):
@@ -146,7 +167,7 @@
     own_block = jnp.einsum(
         "rp,pxnf->xnrf", placer, arrived, preferred_element_type=jnp.float32
     ).astype(jnp.bfloat16)
-    incoming = lax.all_gather(own_block, "blk", axis=2, tiled=True)
+    incoming = ring_gather(own_block, "blk", 2)
     cross_re = jnp.einsum("xnif,xnjf->fij", own_block, incoming, preferred_element_type=jnp.float32)
     cross_im = jnp.einsum(
         "nif,njf->fij", own_block[1], incoming[0], preferred_element_type=jnp.float32

time: 165 us -> 530 us (3.21)
  local copies, waits for them, and re-layouts: 33.8 us -> 407 us
  waiting for transfers between devices: 83.7 us -> 69.4 us
  starting transfers between devices: 8.39 us -> 22.2 us
  matrix products: 16.9 us -> 8.77 us
    dynamic_update_slice x0 -> x8, local copies, waits for them, and re-layouts: none -> 362 us  [the longest x4 195 us: ring_gather(): lax.dynamic_update_slice_in_dim(result, from_left, (index - step) % size...]
    all_gather x1 -> x0, waiting for transfers between devices: 43.8 us -> none  [per_device(): incoming = lax.all_gather(own_block, 'blk', axis=2, tiled=True)]
    ppermute x0 -> x7, local copies, waits for them, and re-layouts: none -> 30.9 us  [the longest x4 17.3 us: ring_gather(): from_left = lax.ppermute(from_left, axis, upward)]
    ppermute x0 -> x7, waiting for transfers between devices: none -> 20.2 us  [the longest x4 13.7 us: ring_gather(): from_left = lax.ppermute(from_left, axis, upward)]
    ppermute x0 -> x7, starting transfers between devices: none -> 14 us  [the longest x3 10.1 us: ring_gather(): from_right = lax.ppermute(from_right, axis, backward)]
    all_gather x1 -> x0, local copies, waits for them, and re-layouts: 12.6 us -> none  [per_device(): incoming = lax.all_gather(own_block, 'blk', axis=2, tiled=True)]
    unnamed x3 -> x2, waiting for transfers between devices: 30.2 us -> 39.5 us
    squeeze x3 -> x0, local copies, waits for them, and re-layouts: 8.58 us -> none  [the longest x2 5.95 us: per_device(): incoming[1]]
  transfers between devices with their start and end apart: 5 -> 11, of which waited for: 5 -> 8; matrix products, arithmetic and copies ran while one was open for 5% -> 66% of each run, Pallas kernels for 0% -> 0%
where the time goes in v1:
time: 530 us; the launch traced here: 529 us
  local copies, waits for them, and re-layouts  407 us (77%)
  waiting for transfers between devices  69.4 us (13%)
  starting transfers between devices  22.2 us (4%)
  between operations  13.8 us (3%)
  matrix products  8.77 us (2%)
  other arithmetic  7.81 us (1%)
    dynamic_update_slice x4, local copies, waits for them, and re-layouts, ring_gather(): lax.dynamic_update_slice_in_dim(result, from_left, (index - step) % size...  195 us
    dynamic_update_slice x3, local copies, waits for them, and re-layouts, ring_gather(): lax.dynamic_update_slice_in_dim(result, from_right, (index + step) % size...  146 us
    unnamed x2, waiting for transfers between devices  39.5 us
    dynamic_update_slice x1, local copies, waits for them, and re-layouts, ring_gather(): result = lax.dynamic_update_slice_in_dim(result, x, index * rows, axis=dim)  20.9 us
    ppermute x4, local copies, waits for them, and re-layouts, ring_gather(): from_left = lax.ppermute(from_left, axis, upward)  17.3 us
    ppermute x4, waiting for transfers between devices, ring_gather(): from_left = lax.ppermute(from_left, axis, upward)  13.7 us
    ppermute x3, local copies, waits for them, and re-layouts, ring_gather(): from_right = lax.ppermute(from_right, axis, backward)  13.6 us
  transfers between devices with their start and end apart: 11, of which 8 were waited for; matrix products, arithmetic and copies ran while one was open for 66% of the time, Pallas kernels for 0%

profile of v1, /device:TPU:0, one launch (start us, length us, event | category | flops | bytes accessed | tf_op | source)
XLA Modules:
  0.0 529.1 jit_solution(6426175619779160591)
XLA Ops:
  7.8 5.0 multiply_convert_fusion.1
  23.4 7.2 %all-to-all-start = ((bf16[8,2,2,32,128]{4,1,3,2,0:T(2,128)(2,1)}), bf16[8,2,2,32,128]{4,1,3,2,0:T(2,128)(2,1)S(1)}, u32[]{:S(2)}, u32[]{:S(2)}) async-start(bf16[8,2,2,32,128]{4,1,3,2,0:T(2,128)(2,1)} %copy.50), calls=%async_computation | async-start | bytes 524288 | tf_op jit(solution)/shard_map/all_to_all | solution.py:161
  30.8 9.0 %all-to-all-done = bf16[8,2,2,32,128]{4,1,3,2,0:T(2,128)(2,1)S(1)} async-done(((bf16[8,2,2,32,128]{4,1,3,2,0:T(2,128)(2,1)}), bf16[8,2,2,32,128]{4,1,3,2,0:T(2,128)(2,1)S(1)}, u32[]{:S(2)}, u32[]{:S(2)}) %all-to-all-start) | async-done | bytes 262176 | tf_op jit(solution)/shard_map/all_to_all | solution.py:161
  45.0 5.6 %collective-permute-done.2 = bf16[2,32,16,128]{3,2,1,0:T(8,128)(2,1)S(1)} collective-permute-done((bf16[2,32,16,128]{3,2,1,0:T(8,128)(2,1)S(1)}, bf16[2,32,16,128]{3,2,1,0:T(8,128)(2,1)S(1)}, u32[]{:S(2)}, u32[]{:S(2)}) %collective-permute-start.2) | collective-permute-done | bytes 262176 | tf_op jit(solution)/shard_map/ppermute | solution.py:25
  53.1 4.3 collective-permute-start.5
  57.3 3.7 collective-permute-done.4
  61.0 6.5 %collective-permute-done.5 = bf16[2,32,16,128]{3,2,1,0:T(8,128)(2,1)} collective-permute-done((bf16[2,32,16,128]{3,2,1,0:T(8,128)(2,1)S(1)}, bf16[2,32,16,128]{3,2,1,0:T(8,128)(2,1)}, u32[]{:S(2)}, u32[]{:S(2)}) %collective-permute-start.5) | collective-permute-done | bytes 262176 | tf_op jit(solution)/shard_map/ppermute | solution.py:30
  70.0 4.4 collective-permute-done.6
  82.4 20.9 %dynamic_update_slice.24 = bf16[2,32,128,128]{2,1,3,0:T(8,128)(2,1)S(1)} dynamic-update-slice(bf16[2,32,128,128]{2,1,3,0:T(8,128)(2,1)S(1)} %broadcast_in_dim.2, bf16[2,32,16,128]{2,1,3,0:T(8,128)(2,1)} %copy.53, s32[]{:T(128)} %constant.176.clone.1, s32[]{:T(128)} %constant.176.clone.1, s32[]{:T(128)S(6)} %select_n.234, s32[]{:T(128)} %constant.176.clone.1) | dynamic-update-slice | bytes 524292 | tf_op jit(solution)/shard_map/dynamic_update_slice | solution.py:21
  103.3 4.5 copy.54
  107.9 48.7 %dynamic_update_slice.25 = bf16[2,32,128,128]{2,1,3,0:T(8,128)(2,1)S(1)} dynamic-update-slice(bf16[2,32,128,128]{2,1,3,0:T(8,128)(2,1)S(1)} %dynamic_update_slice.24, bf16[2,32,16,128]{2,1,3,0:T(8,128)(2,1)} %copy.54, s32[]{:T(128)} %constant.176.clone.1, s32[]{:T(128)} %constant.176.clone.1, s32[]{:T(128)S(6)} %select_n.236, s32[]{:T(128)} %constant.176.clone.1) | dynamic-update-slice | bytes 524292 | tf_op jit(solution)/shard_map/dynamic_update_slice | solution.py:26
  156.5 4.5 copy.55
  161.1 48.7 %dynamic_update_slice.26 = bf16[2,32,128,128]{2,1,3,0:T(8,128)(2,1)S(1)} dynamic-update-slice(bf16[2,32,128,128]{2,1,3,0:T(8,128)(2,1)S(1)} %dynamic_update_slice.25, bf16[2,32,16,128]{2,1,3,0:T(8,128)(2,1)} %copy.55, s32[]{:T(128)} %constant.176.clone.1, s32[]{:T(128)} %constant.176.clone.1, s32[]{:T(128)S(6)} %select_n.238, s32[]{:T(128)} %constant.176.clone.1) | dynamic-update-slice | bytes 524292 | tf_op jit(solution)/shard_map/dynamic_update_slice | solution.py:31
  209.7 4.5 copy.56
  214.3 48.7 %dynamic_update_slice.27 = bf16[2,32,128,128]{2,1,3,0:T(8,128)(2,1)S(1)} dynamic-update-slice(bf16[2,32,128,128]{2,1,3,0:T(8,128)(2,1)S(1)} %dynamic_update_slice.26, bf16[2,32,16,128]{2,1,3,0:T(8,128)(2,1)} %copy.56, s32[]{:T(128)} %constant.176.clone.1, s32[]{:T(128)} %constant.176.clone.1, s32[]{:T(128)S(6)} %select_n.240, s32[]{:T(128)} %constant.176.clone.1) | dynamic-update-slice | bytes 524292 | tf_op jit(solution)/shard_map/dynamic_update_slice | solution.py:26
  262.9 4.5 copy.57
  267.5 48.7 %dynamic_update_slice.28 = bf16[2,32,128,128]{2,1,3,0:T(8,128)(2,1)S(1)} dynamic-update-slice(bf16[2,32,128,128]{2,1,3,0:T(8,128)(2,1)S(1)} %dynamic_update_slice.27, bf16[2,32,16,128]{2,1,3,0:T(8,128)(2,1)} %copy.57, s32[]{:T(128)} %constant.176.clone.1, s32[]{:T(128)} %constant.176.clone.1, s32[]{:T(128)S(6)} %select_n.242, s32[]{:T(128)} %constant.176.clone.1) | dynamic-update-slice | bytes 524292 | tf_op jit(solution)/shard_map/dynamic_update_slice | solution.py:31
  316.1 3.7 copy.58
  319.8 48.7 %dynamic_update_slice.29 = bf16[2,32,128,128]{2,1,3,0:T(8,128)(2,1)S(1)} dynamic-update-slice(bf16[2,32,128,128]{2,1,3,0:T(8,128)(2,1)S(1)} %dynamic_update_slice.28, bf16[2,32,16,128]{2,1,3,0:T(8,128)(2,1)} %copy.58, s32[]{:T(128)} %constant.176.clone.1, s32[]{:T(128)} %constant.176.clone.1, s32[]{:T(128)S(6)} %select_n.244, s32[]{:T(128)} %constant.176.clone.1) | dynamic-update-slice | bytes 524292 | tf_op jit(solution)/shard_map/dynamic_update_slice | solution.py:26
  368.5 4.5 copy.59
  373.0 48.7 %dynamic_update_slice.30 = bf16[2,32,128,128]{2,1,3,0:T(8,128)(2,1)S(1)} dynamic-update-slice(bf16[2,32,128,128]{2,1,3,0:T(8,128)(2,1)S(1)} %dynamic_update_slice.29, bf16[2,32,16,128]{2,1,3,0:T(8,128)(2,1)} %copy.59, s32[]{:T(128)} %constant.176.clone.1, s32[]{:T(128)} %constant.176.clone.1, s32[]{:T(128)S(6)} %select_n.246, s32[]{:T(128)} %constant.176.clone.1) | dynamic-update-slice | bytes 524292 | tf_op jit(solution)/shard_map/dynamic_update_slice | solution.py:31
  421.7 4.5 copy.60
  426.2 48.7 %dynamic_update_slice.31 = bf16[2,32,128,128]{2,1,3,0:T(8,128)(2,1)S(1)} dynamic-update-slice(bf16[2,32,128,128]{2,1,3,0:T(8,128)(2,1)S(1)} %dynamic_update_slice.30, bf16[2,32,16,128]{2,1,3,0:T(8,128)(2,1)} %copy.60, s32[]{:T(128)} %constant.176.clone.1, s32[]{:T(128)} %constant.176.clone.1, s32[]{:T(128)S(6)} %select_n.248, s32[]{:T(128)} %constant.176.clone.1) | dynamic-update-slice | bytes 524292 | tf_op jit(solution)/shard_map/dynamic_update_slice | solution.py:26
  480.3 39.5 %reduce-scatter.5.cloned.1.call-done = f32[64,4096]{1,0:T(8,128)} async-done(((f32[128,4096]{1,0:T(8,128)}), f32[64,4096]{1,0:T(8,128)}) %reduce-scatter.5.cloned.1.call-update) | async-done | bytes 1048592
  (79 shorter events, 37.8 us)
Async XLA Ops:
  6.5 12.6 %copy-start = (f32[128]{0:T(128)S(1)}, f32[128]{0:T(128)}, u32[]{:S(2)}) copy-start(f32[128]{0:T(128)} %param.5) | copy-start | bytes 1540
  7.8 5.0 copy-start.8
  15.6 5.8 %copy-start.6 = (s32[1,8,2]{1,2,0:T(2,128)S(1)}, s32[1,8,2]{1,2,0:T(2,128)}, u32[]{:S(2)}) copy-start(s32[1,8,2]{1,2,0:T(2,128)} %param.6) | copy-start | bytes 196
  18.5 12.1 %copy-start.7 = (s32[1,8,2]{1,2,0:T(2,128)S(1)}, s32[1,8,2]{1,2,0:T(2,128)}, u32[]{:S(2)}) copy-start(s32[1,8,2]{1,2,0:T(2,128)} %param.7) | copy-start | bytes 196
  18.6 1.7 collective-permute-start
  20.5 1.3 collective-permute-start.1
  23.4 16.4 %all-to-all-start = ((bf16[8,2,2,32,128]{4,1,3,2,0:T(2,128)(2,1)}), bf16[8,2,2,32,128]{4,1,3,2,0:T(2,128)(2,1)S(1)}, u32[]{:S(2)}, u32[]{:S(2)}) async-start(bf16[8,2,2,32,128]{4,1,3,2,0:T(2,128)(2,1)} %copy.50), calls=%async_computation | async-start | bytes 524288 | tf_op jit(solution)/shard_map/all_to_all | solution.py:161
  30.6 489.2 %reduce-scatter.5.cloned.1.call-start = ((), (), s32[]{:S(2)}) async-start(), calls=%async_computation.2 | async-start | bytes 3145728
  40.2 10.4 %collective-permute-start.2 = (bf16[2,32,16,128]{3,2,1,0:T(8,128)(2,1)S(1)}, bf16[2,32,16,128]{3,2,1,0:T(8,128)(2,1)S(1)}, u32[]{:S(2)}, u32[]{:S(2)}) collective-permute-start(bf16[2,32,16,128]{3,2,1,0:T(8,128)(2,1)S(1)} %fusion.12), channel_id=1, source_target_pairs={{0,4},{4,8},{8,12},{12,16},{16,20},{20,24},{24,28},{28,0},{1,5},{5... | collective-permute-start | bytes 786440 | tf_op jit(solution)/shard_map/ppermute | solution.py:25
  41.7 11.4 %collective-permute-start.3 = (bf16[2,32,16,128]{3,2,1,0:T(8,128)(2,1)S(1)}, bf16[2,32,16,128]{3,2,1,0:T(8,128)(2,1)S(1)}, u32[]{:S(2)}, u32[]{:S(2)}) collective-permute-start(bf16[2,32,16,128]{3,2,1,0:T(8,128)(2,1)S(1)} %fusion.12), channel_id=1, source_target_pairs={{0,28},{4,0},{8,4},{12,8},{16,12},{20,16},{24,20},{28,24},{1,29},{... | collective-permute-start | bytes 786440 | tf_op jit(solution)/shard_map/ppermute | solution.py:30
  50.6 23.8 %copy-start.5 = (bf16[2,32,16,128]{3,2,1,0:T(8,128)(2,1)}, bf16[2,32,16,128]{3,2,1,0:T(8,128)(2,1)S(1)}, u32[]{:S(2)}) copy-start(bf16[2,32,16,128]{3,2,1,0:T(8,128)(2,1)S(1)} %collective-permute-done.2) | copy-start | bytes 786436
  50.6 10.4 %collective-permute-start.4 = (bf16[2,32,16,128]{3,2,1,0:T(8,128)(2,1)S(1)}, bf16[2,32,16,128]{3,2,1,0:T(8,128)(2,1)S(1)}, u32[]{:S(2)}, u32[]{:S(2)}) collective-permute-start(bf16[2,32,16,128]{3,2,1,0:T(8,128)(2,1)S(1)} %collective-permute-done.2), channel_id=1, source_target_pairs={{0,4},{4,8},{8,12},{12,16},{16,20},{20,24},{24,28},{28,0},{1,5},{5... | collective-permute-start | bytes 786440 | tf_op jit(solution)/shard_map/ppermute | solution.py:25
  53.1 25.0 %copy-start.3 = (bf16[2,32,16,128]{3,2,1,0:T(8,128)(2,1)}, bf16[2,32,16,128]{3,2,1,0:T(8,128)(2,1)S(1)}, u32[]{:S(2)}) copy-start(bf16[2,32,16,128]{3,2,1,0:T(8,128)(2,1)S(1)} %collective-permute-done.3) | copy-start | bytes 786436
  53.1 14.4 %collective-permute-start.5 = (bf16[2,32,16,128]{3,2,1,0:T(8,128)(2,1)S(1)}, bf16[2,32,16,128]{3,2,1,0:T(8,128)(2,1)}, u32[]{:S(2)}, u32[]{:S(2)}) collective-permute-start(bf16[2,32,16,128]{3,2,1,0:T(8,128)(2,1)S(1)} %collective-permute-done.3), channel_id=1, source_target_pairs={{0,28},{4,0},{8,4},{12,8},{16,12},{20,16},{24,20},{28,24},{1,29},{... | collective-permute-start | bytes 786440 | tf_op jit(solution)/shard_map/ppermute | solution.py:30
  61.0 19.8 %copy-start.4 = (bf16[2,32,16,128]{3,2,1,0:T(8,128)(2,1)}, bf16[2,32,16,128]{3,2,1,0:T(8,128)(2,1)S(1)}, u32[]{:S(2)}) copy-start(bf16[2,32,16,128]{3,2,1,0:T(8,128)(2,1)S(1)} %collective-permute-done.4) | copy-start | bytes 786436
  61.0 13.4 %collective-permute-start.6 = (bf16[2,32,16,128]{3,2,1,0:T(8,128)(2,1)S(1)}, bf16[2,32,16,128]{3,2,1,0:T(8,128)(2,1)S(1)}, u32[]{:S(2)}, u32[]{:S(2)}) collective-permute-start(bf16[2,32,16,128]{3,2,1,0:T(8,128)(2,1)S(1)} %collective-permute-done.4), channel_id=1, source_target_pairs={{0,4},{4,8},{8,12},{12,16},{16,20},{20,24},{24,28},{28,0},{1,5},{5... | collective-permute-start | bytes 786440 | tf_op jit(solution)/shard_map/ppermute | solution.py:25
  67.5 300.9 %collective-permute-start.7 = (bf16[2,32,16,128]{3,2,1,0:T(8,128)(2,1)}, bf16[2,32,16,128]{3,2,1,0:T(8,128)(2,1)}, u32[]{:S(2)}, u32[]{:S(2)}) collective-permute-start(bf16[2,32,16,128]{3,2,1,0:T(8,128)(2,1)} %collective-permute-done.5), channel_id=1, source_target_pairs={{0,28},{4,0},{8,4},{12,8},{16,12},{20,16},{24,20},{28,24},{1,29},{... | collective-permute-start | bytes 786440 | tf_op jit(solution)/shard_map/ppermute | solution.py:30
  74.4 347.3 %collective-permute-start.8 = (bf16[2,32,16,128]{3,2,1,0:T(8,128)(2,1)S(1)}, bf16[2,32,16,128]{3,2,1,0:T(8,128)(2,1)}, u32[]{:S(2)}, u32[]{:S(2)}) collective-permute-start(bf16[2,32,16,128]{3,2,1,0:T(8,128)(2,1)S(1)} %collective-permute-done.6), channel_id=1, source_target_pairs={{0,4},{4,8},{8,12},{12,16},{16,20},{20,24},{24,28},{28,0},{1,5},{5... | collective-permute-start | bytes 786440 | tf_op jit(solution)/shard_map/ppermute | solution.py:25
  474.9 1.0 copy-start.1
  474.9 1.5 copy-start.2
Sparse Core Ops, SparseCore 0:
  480.4 39.3 reduce-scatter.4
